TPU v7x, 512 devices: a whole 4x8x8 slice. The times are simulated.
512 devices in a mesh: space: 32 (over y_lo, z), field: 16 (over x, y_hi, core).
Axes of the slice: x: 4, y: 8 (y_hi: 2, y_lo: 4; y = y_hi * 4 + y_lo), z: 8, core: 2. Of those that a mesh axis runs over, the one named last changes fastest.
Arguments:
- fields: float32 [16, 1024, 6144], P('field', 'space'), may hold values from -6 to 6
- zone_ids: int32 [1024, 6144], P('space'), may hold values from 0 to 7
- diffusivity: float32 [16, 8], P('field'), may hold values from 0.3 to 3
- heat_rate: float32 [15], replicated, may hold values from 0.3 to 1.5
- weight_in: bfloat16 [384, 16], replicated, may hold values from -1.5 to 1.5
- bias_in: float32 [384], replicated, may hold values from -3 to 3
- weight_mid: bfloat16 [384, 384], replicated, may hold values from -0.3125 to 0.3125
- bias_mid: float32 [384], replicated, may hold values from -3 to 3
- weight_out: bfloat16 [16, 384], replicated, may hold values from -0.3125 to 0.3125
- bias_out: float32 [16], replicated, may hold values from -2 to 2
Outputs:
- new_fields: float32 [16, 1024, 6144], P('field', 'space')
All inputs are finite; a program needn't handle non-finite values.
Results may differ from a plain program's by a relative error of at most 0.005.
Values may be sent and summed in bfloat16 or wider, within the bound.
No kernel may reach another device: no remote copies, remote signals or barrier semaphores. Data moves between devices by JAX's collectives and lax.ppermute only.
A program may use at most 64 MiB of HBM per device.

v0:
```python
import jax
import jax.numpy as jnp
from jax import lax
from jax.sharding import PartitionSpec as P

FIELDS = 16
SWEEPS = 3
ROWS_BLK = 1024
RELAX_WEIGHTS = (0.8, 1.25, 0.95)


def extended(cells, sides, width):
    for axis, dim in sides:
        count = lax.axis_size(axis)
        ends = count - 1
        head = lax.slice_in_dim(cells, 0, width, axis=dim)
        tail = lax.slice_in_dim(cells, cells.shape[dim] - width, cells.shape[dim], axis=dim)
        cells = jnp.concatenate(
            [
                lax.ppermute(tail, axis, [(i, (i + 1) % count) for i in range(ends)]),
                cells,
                lax.ppermute(head, axis, [((i + 1) % count, i) for i in range(ends)]),
            ],
            axis=dim,
        )
    return cells


def from_root(block, axis, holder):
    block = jnp.where(lax.axis_index(axis) == holder, block, jnp.zeros_like(block))
    return lax.psum(block, axis)


def relax_step(padded, source, coef_pad, weight):
    middle = padded[:, 1:-1]
    coef_mid = coef_pad[:, 1:-1]
    face_north = 0.5 * (coef_mid + coef_pad[:, 2:])
    face_south = 0.5 * (coef_mid + coef_pad[:, :-2])
    face_east = 0.5 * (coef_mid + jnp.roll(coef_mid, -1, 2))
    face_west = 0.5 * (coef_mid + jnp.roll(coef_mid, 1, 2))
    diagonal = 1.0 + face_north + face_south + face_east + face_west
    image = diagonal * middle - face_north * padded[:, 2:] - face_south * padded[:, :-2]
    image = image - face_east * jnp.roll(middle, -1, 2) - face_west * jnp.roll(middle, 1, 2)
    return middle + weight * (source - image) / diagonal


def lookup(zone_ids, diffusivity):
    coefs = jnp.zeros((diffusivity.shape[0],) + zone_ids.shape, jnp.float32)
    for number in range(diffusivity.shape[1]):
        coefs = coefs + jnp.where(
            (zone_ids == number)[None], diffusivity[:, number][:, None, None], jnp.float32(0.0)
        )
    return coefs


def on_device(
    fields,
    zone_ids,
    diffusivity,
    heat_rate,
    weight_in,
    bias_in,
    weight_mid,
    bias_mid,
    weight_out,
    bias_out,
):
    count_here, rows_here, columns = fields.shape
    coefs = lookup(zone_ids, diffusivity)
    stacked = extended(jnp.stack([fields, coefs]), (("space", 2),), 1)
    coef_pad = stacked[1]
    state = relax_step(stacked[0], fields, coef_pad, RELAX_WEIGHTS[0])
    for number in range(1, SWEEPS):
        padded = extended(state, (("space", 1),), 1)
        state = relax_step(padded, fields, coef_pad, RELAX_WEIGHTS[number])
    span = ROWS_BLK * lax.axis_size("field")
    blocks = rows_here * columns // span
    by_block = state.reshape(count_here, blocks, span)

    def one_block(row_block):
        hidden = jax.nn.silu(
            jnp.dot(weight_in, row_block, preferred_element_type=jnp.float32) + bias_in[:, None]
        ).astype(jnp.bfloat16)
        hidden = jax.nn.silu(
            jnp.dot(weight_mid, hidden, preferred_element_type=jnp.float32) + bias_mid[:, None]
        ).astype(jnp.bfloat16)
        return (
            jnp.dot(weight_out, hidden, preferred_element_type=jnp.float32) + bias_out[:, None]
        ).astype(jnp.bfloat16)

    moved = jnp.moveaxis(
        lax.all_to_all(
            by_block.astype(jnp.bfloat16), "field", split_axis=2, concat_axis=0, tiled=True
        ),
        1,
        0,
    )
    change = jnp.moveaxis(lax.map(one_block, moved), 0, 1)
    change = lax.all_to_all(change, "field", split_axis=0, concat_axis=2, tiled=True).astype(
        jnp.float32
    )
    heat_local = by_block[-1] + change[-1]
    heat_new = from_root(heat_local, "field", lax.axis_size("field") - 1)
    first_field = lax.axis_index("field") * count_here
    rate_pad = jnp.concatenate([heat_rate, jnp.zeros((1,), jnp.float32)], 0)
    rate_here = lax.dynamic_slice_in_dim(rate_pad, first_field, count_here)
    factor = jnp.exp(rate_here[:, None, None] * jnp.tanh(heat_new)[None])
    result = by_block + (change * factor).astype(jnp.bfloat16).astype(jnp.float32)
    field_ids = first_field + jnp.arange(count_here, dtype=jnp.int32)
    result = jnp.where((field_ids == FIELDS - 1)[:, None, None], heat_new[None], result)
    return result.reshape(count_here, rows_here, columns)


def solution(mesh):
    return jax.shard_map(
        on_device,
        mesh=mesh,
        in_specs=(
            P("field", "space", None),
            P("space", None),
            P("field", None),
            P(),
            P(),
            P(),
            P(),
            P(),
            P(),
            P(),
        ),
        out_specs=P("field", "space", None),
        check_vma=False,
    )
```

profile of v0, /device:TPU:1, one launch (start us, length us, event | category | flops | bytes accessed | tf_op | source)
XLA Modules:
  0.0 460.7 jit_solution(11899596553922637642)
XLA Ops:
  6.5 1.6 fusion.65
  8.2 6.7 %add_bitcast_fusion = f32[1,1,32,6144]{3,2,1,0:T(8,128)S(1)} fusion(s32[32,6144]{1,0:T(8,128)} %param.13, f32[]{:T(128)} %bitcast.13, f32[]{:T(128)} %bitcast.12, f32[]{:T(128)} %bitcast.11, f32[]{:T(128)} %bitcast.10, f32[]{:T(128)} %bitcast.9, f32[]{:T(128)} %bitcast.8, f32[]{:T(128)} %bitcast.7, f32[]{:T(128)} %bitcast.6), kind=kLoop, calls=%fused_computation.80 | loop fusion | flops 4521984 | bytes 1572896 | tf_op jit(solution)/shard_map/stack | solution.py:70
  14.9 4.8 %collective-permute-start = (f32[2,1,1,6144]{3,2,1,0:T(1,128)S(1)}, f32[2,1,1,6144]{3,2,1,0:T(1,128)S(1)}, u32[]{:S(2)}, u32[]{:S(2)}) collective-permute-start(f32[2,1,1,6144]{3,2,1,0:T(1,128)S(1)} %get-tuple-element.78), channel_id=1, source_target_pairs={{0,16},{16,32},{32,48},{48,64},{64,80},{80,96},{96,112},{112,128},... | collective-permute-start | bytes 147464 | tf_op jit(solution)/shard_map/ppermute | solution.py:20
  19.8 1.3 collective-permute-start.1
  21.1 4.2 collective-permute-done.1
  26.3 1.0 fusion.45
  27.6 1.3 collective-permute-start.2
  28.9 4.6 %collective-permute-start.3 = (f32[1,1,6144]{2,1,0:T(1,128)S(1)}, f32[1,1,6144]{2,1,0:T(1,128)S(1)}, u32[]{:S(2)}, u32[]{:S(2)}) collective-permute-start(f32[1,1,6144]{2,1,0:T(1,128)S(1)} %get-tuple-element.99), channel_id=1, source_target_pairs={{0,16},{16,32},{32,48},{48,64},{64,80},{80,96},{96,112},{112,128},... | collective-permute-start | bytes 73736 | tf_op jit(solution)/shard_map/ppermute | solution.py:20
  33.6 0.9 collective-permute-done.3
  34.4 0.9 fusion.36
  35.6 1.3 collective-permute-start.4
  36.9 6.0 %collective-permute-start.5 = (f32[1,1,6144]{2,1,0:T(1,128)S(1)}, f32[1,1,6144]{2,1,0:T(1,128)S(1)}, u32[]{:S(2)}, u32[]{:S(2)}) collective-permute-start(f32[1,1,6144]{2,1,0:T(1,128)S(1)} %get-tuple-element.89), channel_id=1, source_target_pairs={{0,16},{16,32},{32,48},{48,64},{64,80},{80,96},{96,112},{112,128},... | collective-permute-start | bytes 73736 | tf_op jit(solution)/shard_map/ppermute | solution.py:20
  43.0 0.7 collective-permute-done.5
  43.7 0.9 fusion.51
  45.2 12.8 %copy.13 = bf16[1,12,16384]{1,0,2:T(2,128)(2,1)} copy(bf16[1,12,16384]{2,1,0:T(8,128)(2,1)S(1)} %convert_element_type.50) | data formatting | bytes 786432 | tf_op jit(solution)/shard_map/convert_element_type | solution.py:93
  58.5 90.8 %reduce = bf16[16384,12]{1,0:T(8,128)(2,1)} reduce(bf16[16384,1,12]{2,1,0:T(2,128)(2,1)} %bitcast.109, bf16[]{:T(256)} %broadcast.69), dimensions={1}, to_apply=%bitcast.85.reduce_sub_computation | reduce | bytes 786434
  149.3 9.5 %reshape.89 = bf16[16,2,6144]{2,1,0:T(2,128)(2,1)} reshape(bf16[16384,12]{1,0:T(8,128)(2,1)} %reduce) | data formatting | bytes 786432
  158.9 13.1 %all-to-all-start = ((bf16[16,2,6144]{2,1,0:T(2,128)(2,1)}), bf16[16,2,6144]{2,1,0:T(2,128)(2,1)S(1)}, u32[]{:S(2)}, u32[]{:S(2)}) async-start(bf16[16,2,6144]{2,1,0:T(2,128)(2,1)} %reshape.89), calls=%async_computation | async-start | bytes 786432 | tf_op jit(solution)/shard_map/all_to_all | solution.py:92
  172.0 12.3 %all-to-all-done = bf16[16,2,6144]{2,1,0:T(2,128)(2,1)S(1)} async-done(((bf16[16,2,6144]{2,1,0:T(2,128)(2,1)}), bf16[16,2,6144]{2,1,0:T(2,128)(2,1)S(1)}, u32[]{:S(2)}, u32[]{:S(2)}) %all-to-all-start) | async-done | bytes 393248 | tf_op jit(solution)/shard_map/all_to_all | solution.py:92
  184.3 12.2 %reshape.90 = bf16[16384,1,12]{2,1,0:T(2,128)(2,1)} reshape(bf16[16,2,6144]{2,1,0:T(2,128)(2,1)S(1)} %all-to-all-done) | data formatting | bytes 786432
  196.5 15.4 %copy.14 = bf16[1,12,16384]{2,1,0:T(8,128)(2,1)S(1)} copy(bf16[1,12,16384]{1,0,2:T(2,128)(2,1)} %bitcast.110) | data formatting | bytes 786432 | tf_op jit(solution)/shard_map/all_to_all | solution.py:92
  212.9 19.7 %while.10 = (s32[]{:T(128)}, bf16[12,16,1024]{2,1,0:T(8,128)(2,1)S(1)}, bf16[12,16,1024]{2,1,0:T(8,128)(2,1)S(1)}, bf16[384,16]{0,1:T(8,128)(2,1)S(1)}, f32[384]...) while((s32[]{:T(128)}, ...), condition=%wide.region_1.2_spmd, body=%wide.region_0.1_spmd.sunk | while | flops 331907072 | bytes 1962605 | solution.py:98
  213.5 1.0 fusion.83
  214.5 0.6 fusion.82
  215.1 1.0 fusion.83
  216.1 0.6 fusion.82
  216.8 1.0 fusion.83
  217.8 0.6 fusion.82
  218.4 1.0 fusion.83
  220.1 1.0 fusion.83
  221.1 0.6 fusion.82
  221.7 1.0 fusion.83
  223.4 1.0 fusion.83
  224.4 0.6 fusion.82
  225.0 1.0 fusion.83
  226.6 1.0 fusion.83
  227.6 0.6 fusion.82
  228.3 1.0 fusion.83
  229.9 1.0 fusion.83
  230.9 0.6 fusion.82
  231.6 1.0 fusion.83
  232.6 1.1 copy.22
  233.6 4.5 all-to-all-start.1
  238.5 13.4 %all-to-all-done.1 = bf16[16,12,1024]{2,1,0:T(8,128)(2,1)S(1)} async-done(((bf16[16,12,1024]{2,1,0:T(8,128)(2,1)}), bf16[16,12,1024]{2,1,0:T(8,128)(2,1)S(1)}, u32[]{:S(2)}, u32[]{:S(2)}) %all-to-all-start.1) | async-done | bytes 393248 | tf_op jit(solution)/shard_map/all_to_all | solution.py:99
  253.3 1.1 add_select_fusion.1
  255.0 195.6 %all-reduce.2.cloned.1.call-done = f32[12,16384]{1,0:T(8,128)} async-done(((f32[12,16384]{1,0:T(8,128)}), f32[12,16384]{1,0:T(8,128)}) %all-reduce.2.cloned.1.call-update) | async-done | bytes 786448 | tf_op jit(solution)/shard_map/psum | solution.py:31
  450.6 2.2 add_select_fusion
  452.7 1.1 reshape.86
  (49 shorter events, 9.3 us)
Async XLA Ops:
  6.5 8.3 %copy-start = (f32[1,32,6144]{2,1,0:T(8,128)S(1)}, f32[1,32,6144]{2,1,0:T(8,128)}, u32[]{:S(2)}) copy-start(f32[1,32,6144]{2,1,0:T(8,128)} %param.12) | copy-start | bytes 2359300
  14.9 6.1 %collective-permute-start = (f32[2,1,1,6144]{3,2,1,0:T(1,128)S(1)}, f32[2,1,1,6144]{3,2,1,0:T(1,128)S(1)}, u32[]{:S(2)}, u32[]{:S(2)}) collective-permute-start(f32[2,1,1,6144]{3,2,1,0:T(1,128)S(1)} %get-tuple-element.78), channel_id=1, source_target_pairs={{0,16},{16,32},{32,48},{48,64},{64,80},{80,96},{96,112},{112,128},... | collective-permute-start | bytes 147464 | tf_op jit(solution)/shard_map/ppermute | solution.py:20
  19.8 5.5 %collective-permute-start.1 = (f32[2,1,1,6144]{3,2,1,0:T(1,128)S(1)}, f32[2,1,1,6144]{3,2,1,0:T(1,128)S(1)}, u32[]{:S(2)}, u32[]{:S(2)}) collective-permute-start(f32[2,1,1,6144]{3,2,1,0:T(1,128)S(1)} %get-tuple-element.79), channel_id=1, source_target_pairs={{16,0},{32,16},{48,32},{64,48},{80,64},{96,80},{112,96},{128,112},... | collective-permute-start | bytes 147464 | tf_op jit(solution)/shard_map/ppermute | solution.py:22
  27.6 6.0 %collective-permute-start.2 = (f32[1,1,6144]{2,1,0:T(1,128)S(1)}, f32[1,1,6144]{2,1,0:T(1,128)S(1)}, u32[]{:S(2)}, u32[]{:S(2)}) collective-permute-start(f32[1,1,6144]{2,1,0:T(1,128)S(1)} %get-tuple-element.98), channel_id=1, source_target_pairs={{16,0},{32,16},{48,32},{64,48},{80,64},{96,80},{112,96},{128,112},... | collective-permute-start | bytes 73736 | tf_op jit(solution)/shard_map/ppermute | solution.py:22
  28.9 5.6 %collective-permute-start.3 = (f32[1,1,6144]{2,1,0:T(1,128)S(1)}, f32[1,1,6144]{2,1,0:T(1,128)S(1)}, u32[]{:S(2)}, u32[]{:S(2)}) collective-permute-start(f32[1,1,6144]{2,1,0:T(1,128)S(1)} %get-tuple-element.99), channel_id=1, source_target_pairs={{0,16},{16,32},{32,48},{48,64},{64,80},{80,96},{96,112},{112,128},... | collective-permute-start | bytes 73736 | tf_op jit(solution)/shard_map/ppermute | solution.py:20
  35.6 7.4 %collective-permute-start.4 = (f32[1,1,6144]{2,1,0:T(1,128)S(1)}, f32[1,1,6144]{2,1,0:T(1,128)S(1)}, u32[]{:S(2)}, u32[]{:S(2)}) collective-permute-start(f32[1,1,6144]{2,1,0:T(1,128)S(1)} %get-tuple-element.88), channel_id=1, source_target_pairs={{16,0},{32,16},{48,32},{64,48},{80,64},{96,80},{112,96},{128,112},... | collective-permute-start | bytes 73736 | tf_op jit(solution)/shard_map/ppermute | solution.py:22
  36.9 6.8 %collective-permute-start.5 = (f32[1,1,6144]{2,1,0:T(1,128)S(1)}, f32[1,1,6144]{2,1,0:T(1,128)S(1)}, u32[]{:S(2)}, u32[]{:S(2)}) collective-permute-start(f32[1,1,6144]{2,1,0:T(1,128)S(1)} %get-tuple-element.89), channel_id=1, source_target_pairs={{0,16},{16,32},{32,48},{48,64},{64,80},{80,96},{96,112},{112,128},... | collective-permute-start | bytes 73736 | tf_op jit(solution)/shard_map/ppermute | solution.py:20
  158.9 25.4 %all-to-all-start = ((bf16[16,2,6144]{2,1,0:T(2,128)(2,1)}), bf16[16,2,6144]{2,1,0:T(2,128)(2,1)S(1)}, u32[]{:S(2)}, u32[]{:S(2)}) async-start(bf16[16,2,6144]{2,1,0:T(2,128)(2,1)} %reshape.89), calls=%async_computation | async-start | bytes 786432 | tf_op jit(solution)/shard_map/all_to_all | solution.py:92
  211.9 1.0 copy-start.1
  211.9 1.0 copy-start.2
  211.9 0.9 copy-start.3
  211.9 0.9 copy-start.4
  211.9 0.9 copy-start.5
  212.0 0.9 copy-start.6
  233.6 18.3 %all-to-all-start.1 = ((bf16[16,12,1024]{2,1,0:T(8,128)(2,1)}), bf16[16,12,1024]{2,1,0:T(8,128)(2,1)S(1)}, u32[]{:S(2)}, u32[]{:S(2)}) async-start(bf16[16,12,1024]{2,1,0:T(8,128)(2,1)} %bitcast.92), calls=%async_computation.1 | async-start | bytes 1048576 | tf_op jit(solution)/shard_map/all_to_all | solution.py:99
  238.2 212.4 %all-reduce.2.cloned.1.call-start = ((), (), s32[]{:S(2)}) async-start(), calls=%async_computation.2 | async-start | bytes 2097152 | tf_op jit(solution)/shard_map/psum | solution.py:31
  253.2 1.1 copy-start.7
Sparse Core Ops, SparseCore 0:
  254.5 196.0 all-reduce.1
where the time goes:
time: 462 us; the launch traced here: 461 us
  waiting for transfers between devices  227 us (49%)
  other arithmetic  104 us (23%)
  local copies, waits for them, and re-layouts  59.4 us (13%)
  starting transfers between devices  37 us (8%)
  matrix products  19.6 us (4%)
  between operations  13.7 us (3%)
    psum x1, waiting for transfers between devices, from_root(): return lax.psum(block, axis)  196 us
    unnamed x1, other arithmetic  90.8 us
    unnamed x22, local copies, waits for them, and re-layouts  23.9 us
    ppermute x3, starting transfers between devices, extended(): lax.ppermute(tail, axis, [(i, (i + 1) % count) for i in range(ends)])  15.5 us
    all_to_all x1, local copies, waits for them, and re-layouts, on_device(): lax.all_to_all(by_block.astype(jnp.bfloat16), 'field', split_axis=2, conc...  15.4 us
    all_to_all x1, waiting for transfers between devices, on_device(): lax.all_to_all(change, 'field', split_axis=0, concat_axis=2, tiled=True)  13.4 us
    convert_element_type x2, local copies, waits for them, and re-layouts, on_device(): by_block.astype(jnp.bfloat16)  13.4 us
    all_to_all x1, starting transfers between devices, on_device(): lax.all_to_all(by_block.astype(jnp.bfloat16), 'field', split_axis=2, conc...  13.1 us
  transfers between devices with their start and end apart: 9, of which 6 were waited for; matrix products, arithmetic and copies ran while one was open for 0% of the time, Pallas kernels for 0%

commit v1 on v0

--- a/solution.py
+++ b/solution.py
@@ -88,13 +88,16 @@
             jnp.dot(weight_out, hidden, preferred_element_type=jnp.float32) + bias_out[:, None]
         ).astype(jnp.bfloat16)
 
-    moved = jnp.moveaxis(
+    _draw_levels_all = lambda packet: jnp.concatenate(
         lax.all_to_all(
-            by_block.astype(jnp.bfloat16), "field", split_axis=2, concat_axis=0, tiled=True
+            jnp.stack(jnp.split(packet, lax.axis_size("field"), 2), 0),
+            axis_name="field",
+            split_axis=0,
+            concat_axis=0,
         ),
-        1,
         0,
     )
+    moved = jnp.moveaxis(_draw_levels_all(by_block.astype(jnp.bfloat16)), 1, 0)
     change = jnp.moveaxis(lax.map(one_block, moved), 0, 1)
     change = lax.all_to_all(change, "field", split_axis=0, concat_axis=2, tiled=True).astype(
         jnp.float32

time: 462 us -> 330 us (0.71)
  other arithmetic: 104 us -> 13.2 us
  local copies, waits for them, and re-layouts: 59.4 us -> 18.1 us
    unnamed x1 -> x0, other arithmetic: 90.8 us -> none
    all_to_all x1 -> x0, local copies, waits for them, and re-layouts: 15.4 us -> none  [on_device(): lax.all_to_all(by_block.astype(jnp.bfloat16), 'field', split_axis=2, conc...]
    unnamed x22 -> x33, local copies, waits for them, and re-layouts: 23.9 us -> 10 us
    convert_element_type x2 -> x1, local copies, waits for them, and re-layouts: 13.4 us -> 0.59 us  [on_device(): moved = jnp.moveaxis(_draw_levels_all(by_block.astype(jnp.bfloat16)), 1, 0)]
where the time goes in v1:
time: 330 us
  waiting for transfers between devices  228 us (69%)
  starting transfers between devices  36.8 us (11%)
  matrix products  19.5 us (6%)
  local copies, waits for them, and re-layouts  18.1 us (5%)
  between operations  13.7 us (4%)
  other arithmetic  13.2 us (4%)
    psum x1, waiting for transfers between devices, from_root(): return lax.psum(block, axis)  195 us
    ppermute x3, starting transfers between devices, extended(): lax.ppermute(tail, axis, [(i, (i + 1) % count) for i in range(ends)])  15.3 us
    all_to_all x1, waiting for transfers between devices, on_device(): lax.all_to_all(jnp.stack(jnp.split(packet, lax.axis_size('field'), 2), 0)...  13.7 us
    all_to_all x1, waiting for transfers between devices, on_device(): lax.all_to_all(change, 'field', split_axis=0, concat_axis=2, tiled=True)  13.4 us
    all_to_all x1, starting transfers between devices, on_device(): lax.all_to_all(jnp.stack(jnp.split(packet, lax.axis_size('field'), 2), 0)...  13.1 us
    dot_general x12, matrix products, one_block(): jnp.dot(weight_out, hidden, preferred_element_type=jnp.float32)  11.9 us
    unnamed x33, local copies, waits for them, and re-layouts  10 us
    dot_general x12, matrix products, one_block(): jnp.dot(weight_in, row_block, preferred_element_type=jnp.float32)  7.57 us
  transfers between devices with their start and end apart: 9, of which 6 were waited for; matrix products, arithmetic and copies ran while one was open for 0% of the time, Pallas kernels for 0%

profile of v1, /device:TPU:1, one launch (start us, length us, event | category | flops | bytes accessed | tf_op | source)
XLA Modules:
  0.0 329.8 jit_solution(1656951999660638402)
XLA Ops:
  6.5 1.6 fusion.65
  8.2 6.6 %add_bitcast_fusion = f32[1,1,32,6144]{3,2,1,0:T(8,128)S(1)} fusion(s32[32,6144]{1,0:T(8,128)} %param.13, f32[]{:T(128)} %bitcast.13, f32[]{:T(128)} %bitcast.12, f32[]{:T(128)} %bitcast.11, f32[]{:T(128)} %bitcast.10, f32[]{:T(128)} %bitcast.9, f32[]{:T(128)} %bitcast.8, f32[]{:T(128)} %bitcast.7, f32[]{:T(128)} %bitcast.6), kind=kLoop, calls=%fused_computation.80 | loop fusion | flops 4521984 | bytes 1572896 | tf_op jit(solution)/shard_map/stack | solution.py:70
  14.9 4.8 %collective-permute-start = (f32[2,1,1,6144]{3,2,1,0:T(1,128)S(1)}, f32[2,1,1,6144]{3,2,1,0:T(1,128)S(1)}, u32[]{:S(2)}, u32[]{:S(2)}) collective-permute-start(f32[2,1,1,6144]{3,2,1,0:T(1,128)S(1)} %get-tuple-element.105), channel_id=1, source_target_pairs={{0,16},{16,32},{32,48},{48,64},{64,80},{80,96},{96,112},{112,128},... | collective-permute-start | bytes 147464 | tf_op jit(solution)/shard_map/ppermute | solution.py:20
  19.7 1.3 collective-permute-start.1
  21.0 4.2 %collective-permute-done.1 = f32[2,1,1,6144]{3,2,1,0:T(1,128)S(1)} collective-permute-done((f32[2,1,1,6144]{3,2,1,0:T(1,128)S(1)}, f32[2,1,1,6144]{3,2,1,0:T(1,128)S(1)}, u32[]{:S(2)}, u32[]{:S(2)}) %collective-permute-start.1) | collective-permute-done | bytes 49184 | tf_op jit(solution)/shard_map/ppermute | solution.py:22
  26.2 1.0 fusion.45
  27.6 1.3 collective-permute-start.2
  28.9 4.6 %collective-permute-start.3 = (f32[1,1,6144]{2,1,0:T(1,128)S(1)}, f32[1,1,6144]{2,1,0:T(1,128)S(1)}, u32[]{:S(2)}, u32[]{:S(2)}) collective-permute-start(f32[1,1,6144]{2,1,0:T(1,128)S(1)} %get-tuple-element.126), channel_id=1, source_target_pairs={{0,16},{16,32},{32,48},{48,64},{64,80},{80,96},{96,112},{112,128},... | collective-permute-start | bytes 73736 | tf_op jit(solution)/shard_map/ppermute | solution.py:20
  33.6 0.9 collective-permute-done.3
  34.4 0.9 fusion.36
  35.6 1.3 collective-permute-start.4
  36.9 5.8 %collective-permute-start.5 = (f32[1,1,6144]{2,1,0:T(1,128)S(1)}, f32[1,1,6144]{2,1,0:T(1,128)S(1)}, u32[]{:S(2)}, u32[]{:S(2)}) collective-permute-start(f32[1,1,6144]{2,1,0:T(1,128)S(1)} %get-tuple-element.116), channel_id=1, source_target_pairs={{0,16},{16,32},{32,48},{48,64},{64,80},{80,96},{96,112},{112,128},... | collective-permute-start | bytes 73736 | tf_op jit(solution)/shard_map/ppermute | solution.py:20
  42.8 0.9 collective-permute-done.5
  43.7 0.9 fusion.51
  45.3 0.6 constant_dynamic-update-slice_fusion.15
  55.1 13.1 %all-to-all-start = ((bf16[16,1,12,1024]{3,2,1,0:T(8,128)(2,1)}), bf16[16,1,12,1024]{3,2,1,0:T(8,128)(2,1)S(1)}, u32[]{:S(2)}, u32[]{:S(2)}) async-start(bf16[16,1,12,1024]{3,2,1,0:T(8,128)(2,1)} %constant_dynamic-update-slice_fusion), calls=%async_computation | async-start | bytes 1048576 | tf_op jit(solution)/shard_map/all_to_all | solution.py:92
  68.2 13.7 %all-to-all-done = bf16[16,1,12,1024]{3,2,1,0:T(8,128)(2,1)S(1)} async-done(((bf16[16,1,12,1024]{3,2,1,0:T(8,128)(2,1)}), bf16[16,1,12,1024]{3,2,1,0:T(8,128)(2,1)S(1)}, u32[]{:S(2)}, u32[]{:S(2)}) %all-to-all-start) | async-done | bytes 393248 | tf_op jit(solution)/shard_map/all_to_all | solution.py:92
  82.2 19.6 %while.10 = (s32[]{:T(128)}, bf16[12,16,1024]{2,1,0:T(8,128)(2,1)S(1)}, bf16[12,16,1024]{2,1,0:T(8,128)(2,1)S(1)}, bf16[384,16]{0,1:T(8,128)(2,1)S(1)}, f32[384]...) while((s32[]{:T(128)}, ...), condition=%wide.region_1.2_spmd, body=%wide.region_0.1_spmd.sunk | while | flops 331907072 | bytes 1962605 | solution.py:101
  82.9 1.0 fusion.83
  83.8 0.6 fusion.82
  84.5 1.0 fusion.83
  85.5 0.6 fusion.82
  86.1 1.0 fusion.83
  87.1 0.6 fusion.82
  87.8 1.0 fusion.83
  88.7 0.6 fusion.82
  89.4 1.0 fusion.83
  90.4 0.6 fusion.82
  91.0 1.0 fusion.83
  92.0 0.6 fusion.82
  92.7 1.0 fusion.83
  93.6 0.6 fusion.82
  94.3 1.0 fusion.83
  95.3 0.6 fusion.82
  95.9 1.0 fusion.83
  96.9 0.6 fusion.82
  97.6 1.0 fusion.83
  98.5 0.6 fusion.82
  99.2 1.0 fusion.83
  100.2 0.6 fusion.82
  100.8 1.0 fusion.83
  101.8 1.1 copy.36
  102.9 4.5 %all-to-all-start.1 = ((bf16[16,12,1024]{2,1,0:T(8,128)(2,1)}), bf16[16,12,1024]{2,1,0:T(8,128)(2,1)S(1)}, u32[]{:S(2)}, u32[]{:S(2)}) async-start(bf16[16,12,1024]{2,1,0:T(8,128)(2,1)} %bitcast.145), calls=%async_computation.1 | async-start | bytes 1048576 | tf_op jit(solution)/shard_map/all_to_all | solution.py:102
  107.8 13.4 %all-to-all-done.1 = bf16[16,12,1024]{2,1,0:T(8,128)(2,1)S(1)} async-done(((bf16[16,12,1024]{2,1,0:T(8,128)(2,1)}), bf16[16,12,1024]{2,1,0:T(8,128)(2,1)S(1)}, u32[]{:S(2)}, u32[]{:S(2)}) %all-to-all-start.1) | async-done | bytes 393248 | tf_op jit(solution)/shard_map/all_to_all | solution.py:102
  122.5 1.1 add_select_fusion.1
  124.3 195.4 %all-reduce.2.cloned.1.call-done = f32[12,16384]{1,0:T(8,128)} async-done(((f32[12,16384]{1,0:T(8,128)}), f32[12,16384]{1,0:T(8,128)}) %all-reduce.2.cloned.1.call-update) | async-done | bytes 786448 | tf_op jit(solution)/shard_map/psum | solution.py:31
  319.7 2.2 add_select_fusion
  321.9 1.1 reshape.90
  (58 shorter events, 14.9 us)
Async XLA Ops:
  6.5 8.3 %copy-start = (f32[1,32,6144]{2,1,0:T(8,128)S(1)}, f32[1,32,6144]{2,1,0:T(8,128)}, u32[]{:S(2)}) copy-start(f32[1,32,6144]{2,1,0:T(8,128)} %param.12) | copy-start | bytes 2359300
  14.9 6.1 %collective-permute-start = (f32[2,1,1,6144]{3,2,1,0:T(1,128)S(1)}, f32[2,1,1,6144]{3,2,1,0:T(1,128)S(1)}, u32[]{:S(2)}, u32[]{:S(2)}) collective-permute-start(f32[2,1,1,6144]{3,2,1,0:T(1,128)S(1)} %get-tuple-element.105), channel_id=1, source_target_pairs={{0,16},{16,32},{32,48},{48,64},{64,80},{80,96},{96,112},{112,128},... | collective-permute-start | bytes 147464 | tf_op jit(solution)/shard_map/ppermute | solution.py:20
  19.7 5.5 %collective-permute-start.1 = (f32[2,1,1,6144]{3,2,1,0:T(1,128)S(1)}, f32[2,1,1,6144]{3,2,1,0:T(1,128)S(1)}, u32[]{:S(2)}, u32[]{:S(2)}) collective-permute-start(f32[2,1,1,6144]{3,2,1,0:T(1,128)S(1)} %get-tuple-element.106), channel_id=1, source_target_pairs={{16,0},{32,16},{48,32},{64,48},{80,64},{96,80},{112,96},{128,112},... | collective-permute-start | bytes 147464 | tf_op jit(solution)/shard_map/ppermute | solution.py:22
  27.6 6.0 %collective-permute-start.2 = (f32[1,1,6144]{2,1,0:T(1,128)S(1)}, f32[1,1,6144]{2,1,0:T(1,128)S(1)}, u32[]{:S(2)}, u32[]{:S(2)}) collective-permute-start(f32[1,1,6144]{2,1,0:T(1,128)S(1)} %get-tuple-element.125), channel_id=1, source_target_pairs={{16,0},{32,16},{48,32},{64,48},{80,64},{96,80},{112,96},{128,112},... | collective-permute-start | bytes 73736 | tf_op jit(solution)/shard_map/ppermute | solution.py:22
  28.9 5.6 %collective-permute-start.3 = (f32[1,1,6144]{2,1,0:T(1,128)S(1)}, f32[1,1,6144]{2,1,0:T(1,128)S(1)}, u32[]{:S(2)}, u32[]{:S(2)}) collective-permute-start(f32[1,1,6144]{2,1,0:T(1,128)S(1)} %get-tuple-element.126), channel_id=1, source_target_pairs={{0,16},{16,32},{32,48},{48,64},{64,80},{80,96},{96,112},{112,128},... | collective-permute-start | bytes 73736 | tf_op jit(solution)/shard_map/ppermute | solution.py:20
  35.6 7.2 %collective-permute-start.4 = (f32[1,1,6144]{2,1,0:T(1,128)S(1)}, f32[1,1,6144]{2,1,0:T(1,128)S(1)}, u32[]{:S(2)}, u32[]{:S(2)}) collective-permute-start(f32[1,1,6144]{2,1,0:T(1,128)S(1)} %get-tuple-element.115), channel_id=1, source_target_pairs={{16,0},{32,16},{48,32},{64,48},{80,64},{96,80},{112,96},{128,112},... | collective-permute-start | bytes 73736 | tf_op jit(solution)/shard_map/ppermute | solution.py:22
  36.9 6.8 %collective-permute-start.5 = (f32[1,1,6144]{2,1,0:T(1,128)S(1)}, f32[1,1,6144]{2,1,0:T(1,128)S(1)}, u32[]{:S(2)}, u32[]{:S(2)}) collective-permute-start(f32[1,1,6144]{2,1,0:T(1,128)S(1)} %get-tuple-element.116), channel_id=1, source_target_pairs={{0,16},{16,32},{32,48},{48,64},{64,80},{80,96},{96,112},{112,128},... | collective-permute-start | bytes 73736 | tf_op jit(solution)/shard_map/ppermute | solution.py:20
  45.2 37.0 %copy-start.1 = (bf16[384,384]{1,0:T(8,128)(2,1)S(1)}, bf16[384,384]{1,0:T(8,128)(2,1)}, u32[]{:S(2)}) copy-start(bf16[384,384]{1,0:T(8,128)(2,1)} %param.18) | copy-start | bytes 884740
  45.2 37.0 %copy-start.2 = (bf16[384,16]{0,1:T(8,128)(2,1)S(1)}, bf16[384,16]{0,1:T(8,128)(2,1)}, u32[]{:S(2)}) copy-start(bf16[384,16]{0,1:T(8,128)(2,1)} %param.16) | copy-start | bytes 36868
  45.2 37.0 %copy-start.3 = (bf16[16,384]{1,0:T(8,128)(2,1)S(1)}, bf16[16,384]{1,0:T(8,128)(2,1)}, u32[]{:S(2)}) copy-start(bf16[16,384]{1,0:T(8,128)(2,1)} %param.20) | copy-start | bytes 36868
  45.2 37.0 %copy-start.4 = (f32[384]{0:T(512)S(1)}, f32[384]{0:T(512)}, u32[]{:S(2)}) copy-start(f32[384]{0:T(512)} %param.17) | copy-start | bytes 4612
  45.2 37.0 %copy-start.5 = (f32[384]{0:T(512)S(1)}, f32[384]{0:T(512)}, u32[]{:S(2)}) copy-start(f32[384]{0:T(512)} %param.19) | copy-start | bytes 4612
  45.2 37.0 %copy-start.6 = (f32[16]{0:T(128)S(1)}, f32[16]{0:T(128)}, u32[]{:S(2)}) copy-start(f32[16]{0:T(128)} %param.21) | copy-start | bytes 196
  55.1 26.8 %all-to-all-start = ((bf16[16,1,12,1024]{3,2,1,0:T(8,128)(2,1)}), bf16[16,1,12,1024]{3,2,1,0:T(8,128)(2,1)S(1)}, u32[]{:S(2)}, u32[]{:S(2)}) async-start(bf16[16,1,12,1024]{3,2,1,0:T(8,128)(2,1)} %constant_dynamic-update-slice_fusion), calls=%async_computation | async-start | bytes 1048576 | tf_op jit(solution)/shard_map/all_to_all | solution.py:92
  102.9 18.3 %all-to-all-start.1 = ((bf16[16,12,1024]{2,1,0:T(8,128)(2,1)}), bf16[16,12,1024]{2,1,0:T(8,128)(2,1)S(1)}, u32[]{:S(2)}, u32[]{:S(2)}) async-start(bf16[16,12,1024]{2,1,0:T(8,128)(2,1)} %bitcast.145), calls=%async_computation.1 | async-start | bytes 1048576 | tf_op jit(solution)/shard_map/all_to_all | solution.py:102
  107.4 212.3 %all-reduce.2.cloned.1.call-start = ((), (), s32[]{:S(2)}) async-start(), calls=%async_computation.2 | async-start | bytes 2097152 | tf_op jit(solution)/shard_map/psum | solution.py:31
  122.5 1.1 copy-start.7
Sparse Core Ops, SparseCore 0:
  123.7 195.9 all-reduce.1
